TPU v7x, 32 devices: a whole 2x2x4 slice. The times are simulated.
32 devices in a mesh: seq: 8 (over y, x, core), chan: 4 (over z).
Axes of the slice: x: 2, y: 2, z: 4, core: 2. Of those that a mesh axis runs over, the one named last changes fastest.
Arguments:
- query_proj: bfloat16 [1024, 8192], P('seq', 'chan'), may hold values from -8 to 8
- key_proj: bfloat16 [1024, 8192], P('seq', 'chan'), may hold values from -8 to 8
- value_proj: bfloat16 [1024, 8192], P('seq', 'chan'), may hold values from -6 to 6
- residual: bfloat16 [1024, 8192], P('seq', 'chan'), may hold values from -6 to 6
- out_weight: bfloat16 [8192, 8192], P('chan', 'seq'), may hold values from -0.0625 to 0.0625
Outputs:
- attn_out: bfloat16 [1024, 8192], P('seq', 'chan')
All inputs are finite; a program needn't handle non-finite values.
Results may differ from a plain program's by a relative error of at most 0.008.
Values may be sent and summed in bfloat16 or wider, within the bound.
No kernel may reach another device: no remote copies, remote signals or barrier semaphores. Data moves between devices by JAX's collectives and lax.ppermute only.
A program may use at most 64 MiB of HBM per device.

v0:
```python
import math
import jax
import jax.numpy as jnp
from jax import lax
from jax.sharding import PartitionSpec as P

HEAD_DIM = 128


def attend(state, query_rows, first_pos, key_block, value_block, block_start, score_scale):
    row_max, row_total, accum = state
    scores = (
        jnp.einsum("qhd,khd->hqk", query_rows, key_block, preferred_element_type=jnp.float32)
        * score_scale
    )
    row_pos = first_pos + jnp.arange(query_rows.shape[0], dtype=jnp.int32)
    col_pos = block_start + jnp.arange(key_block.shape[0], dtype=jnp.int32)
    allowed = (col_pos[None, :] <= row_pos[:, None])[None]
    scores = jnp.where(allowed, scores, -1e30)
    new_max = jnp.maximum(row_max, jnp.max(scores, axis=-1))
    weights = jnp.where(allowed, jnp.exp(scores - new_max[..., None]), 0.0)
    factor = jnp.exp(row_max - new_max)
    row_total = row_total * factor + jnp.sum(weights, axis=-1)
    accum = accum * factor[..., None] + jnp.einsum(
        "hqk,khd->hqd",
        weights.astype(jnp.bfloat16),
        value_block,
        preferred_element_type=jnp.float32,
    )
    return (new_max, row_total, accum)


def guarded(state, query_rows, first_pos, key_block, value_block, block_start, score_scale):
    last_pos = first_pos + query_rows.shape[0] - 1

    def do_update(inner):
        return attend(
            inner, query_rows, first_pos, key_block, value_block, block_start, score_scale
        )

    def keep_state(inner):
        return inner

    return lax.cond(block_start <= last_pos, do_update, keep_state, state)


def per_device(query_proj, key_proj, value_proj, residual, out_weight):
    seg_rows = query_proj.shape[0]
    feat_width = query_proj.shape[1]
    heads_here = feat_width // HEAD_DIM
    seq_count = lax.axis_size("seq")
    chan_count = lax.axis_size("chan")
    segment = lax.axis_index("seq")
    score_scale = 1.0 / math.sqrt(HEAD_DIM)
    groups = [(query_proj, segment * seg_rows)]
    shaped = [
        (rows.reshape(rows.shape[0], heads_here, HEAD_DIM), first_pos) for rows, first_pos in groups
    ]
    starting = tuple(
        (
            (
                jnp.full((heads_here, rows.shape[0]), -1e30, jnp.float32),
                jnp.zeros((heads_here, rows.shape[0]), jnp.float32),
                jnp.zeros((heads_here, rows.shape[0], HEAD_DIM), jnp.float32),
            )
            for rows, first_pos in shaped
        )
    )
    piece_keys = lax.all_gather(key_proj, "seq", axis=0, tiled=True)
    piece_values = lax.all_gather(value_proj, "seq", axis=0, tiled=True)
    piece_rows = piece_keys.shape[0]

    def one_block(block_index, states):
        offset = block_index * seg_rows
        key_block = lax.dynamic_slice_in_dim(piece_keys, offset, seg_rows, 0).reshape(
            seg_rows, heads_here, HEAD_DIM
        )
        value_block = lax.dynamic_slice_in_dim(piece_values, offset, seg_rows, 0).reshape(
            seg_rows, heads_here, HEAD_DIM
        )
        updated = []
        for (query_rows, first_pos), state in zip(shaped, states):
            updated.append(
                guarded(state, query_rows, first_pos, key_block, value_block, offset, score_scale)
            )
        return tuple(updated)

    finals = lax.fori_loop(0, piece_rows // seg_rows, one_block, starting)
    pieces_out = []
    for row_max, row_total, accum in finals:
        ratio = accum / row_total[..., None]
        pieces_out.append(
            ratio.transpose(1, 0, 2).reshape(ratio.shape[1], feat_width).astype(jnp.bfloat16)
        )
    local_context = pieces_out[0]
    gathered = lax.all_gather(local_context, "seq", axis=0, tiled=True)
    sub_rows = seg_rows // chan_count
    grid = gathered.reshape(seq_count, chan_count, sub_rows, feat_width)
    block_tokens = seq_count * sub_rows
    rows = grid.transpose(1, 0, 2, 3).reshape(block_tokens * lax.axis_size("chan"), feat_width)
    partial_sums = lax.psum_scatter(
        jnp.dot(rows, out_weight, preferred_element_type=jnp.float32).astype(jnp.bfloat16),
        "chan",
        scatter_dimension=0,
        tiled=True,
    ).astype(jnp.float32)
    relaid = lax.all_to_all(
        lax.all_to_all(
            partial_sums.astype(jnp.bfloat16), "seq", split_axis=0, concat_axis=1, tiled=True
        ),
        "chan",
        split_axis=1,
        concat_axis=0,
        tiled=True,
    ).astype(partial_sums.dtype)
    return (residual.astype(jnp.float32) + relaid).astype(jnp.bfloat16)


def solution(mesh):
    placed = (
        P("seq", "chan"),
        P("seq", "chan"),
        P("seq", "chan"),
        P("seq", "chan"),
        P("chan", "seq"),
    )
    return jax.shard_map(
        per_device, mesh=mesh, in_specs=placed, out_specs=P("seq", "chan"), check_vma=False
    )
```

profile of v0, /device:TPU:0, one launch (start us, length us, event | category | flops | bytes accessed | tf_op | source)
XLA Modules:
  0.0 250.2 jit_solution(13693621716920695424)
XLA Ops:
  6.5 2.0 copy.32
  8.7 2.1 copy.34
  10.8 1.3 copy.33
  12.4 37.0 %all-gather.4.cloned.1.call-done = bf16[1024,2048]{0,1:T(8,128)(2,1)} async-done(((bf16[128,2048]{0,1:T(8,128)(2,1)}), bf16[1024,2048]{0,1:T(8,128)(2,1)}) %all-gather.4.cloned.1.call-update) | async-done | bytes 4194320 | tf_op jit(solution)/shard_map/all_gather | solution.py:69
  49.4 39.3 %all-gather.6.cloned.1.call-done = bf16[1024,2048]{0,1:T(8,128)(2,1)} async-done(((bf16[128,2048]{0,1:T(8,128)(2,1)}), bf16[1024,2048]{0,1:T(8,128)(2,1)}) %all-gather.6.cloned.1.call-update) | async-done | bytes 4194320 | tf_op jit(solution)/shard_map/all_gather | solution.py:70
  88.9 3.3 %while.19 = (s32[]{:T(128)}, f32[16,128]{1,0:T(8,128)S(1)}, f32[16,128]{1,0:T(8,128)S(1)}, f32[16,128,128]{2,1,0:T(8,128)S(1)}, s32[]{:T(128)}, /*index=5*/s32[]...) while((s32[]{:T(128)}, f32[16,128]{1,0:T(8,128)S(1)}, ...), condition=%wide.region_5.6_spmd, body=%wide.region_0.5_spmd.sunk | while | flops 137122048 | bytes 9111853 | solution.py:88
  88.9 3.0 %conditional.2 = ((f32[16,128]{1,0:T(8,128)S(1)}, f32[16,128]{1,0:T(8,128)S(1)}, f32[16,128,128]{2,1,0:T(8,128)S(1)})) conditional(s32[]{:T(128)} %convert_element_type.63, (f32[16,128]{1,0:T(8,128)S(1)}, f32[16,128]{1,0:T(8,128)S(1)}, f32[16,128,128]{2,1,0:T(8,128)S(1)}) %tuple.61, (s32[]{:T(128)}, s32[]{:T(128)}, bf16[1024,2048]{0,1:T(8,128)(2,1)}, ...), branch_computations={%region_1.0_spmd, %region_2.4_spmd} | conditional | flops 137122048 | bytes 9111630 | solution.py:44
  88.9 1.3 constant_dynamic-slice_fusion
  90.3 0.5 fusion.10
  91.1 0.8 convolution_add_fusion
  92.2 0.3 copy.36
  92.5 0.9 divide_convert_fusion
  93.5 58.4 %all-gather.8.cloned.1.call-done = bf16[1024,2048]{0,1:T(8,128)(2,1)} async-done(((bf16[128,2048]{0,1:T(8,128)(2,1)}), bf16[1024,2048]{0,1:T(8,128)(2,1)}) %all-gather.8.cloned.1.call-update) | async-done | bytes 4194320 | tf_op jit(solution)/shard_map/all_gather | solution.py:96
  151.9 6.5 %copy.37 = bf16[1024,2048]{1,0:T(8,128)(2,1)} copy(bf16[1024,2048]{0,1:T(8,128)(2,1)} %all-gather.8.cloned.1.call-done) | data formatting | bytes 8388608 | tf_op jit(solution)/shard_map/all_gather | solution.py:96
  158.4 2.7 %copy.38 = bf16[4,8,32,2048]{3,2,1,0:T(8,128)(2,1)S(1)} copy(bf16[4,8,32,2048]{3,2,0,1:T(8,128)(2,1)} %bitcast.29) | data formatting | bytes 8388608 | tf_op jit(solution)/shard_map/transpose | solution.py:100
  161.1 0.8 copy-done.1
  161.9 5.7 %convolution_convert_fusion = bf16[1024,1024]{1,0:T(8,128)(2,1)} fusion(bf16[1024,2048]{1,0:T(8,128)(2,1)S(1)} %bitcast.30, bf16[2048,1024]{1,0:T(8,128)(2,1)S(1)} %copy-done.1), kind=kOutput, calls=%fused_computation.18 | convolution fusion | flops 4296015872 | bytes 10485760 | tf_op jit(solution)/shard_map/dot_general | solution.py:102
  167.7 44.0 %reduce-scatter.2.cloned.1.call-done = bf16[256,1024]{1,0:T(8,128)(2,1)} async-done(((bf16[1024,1024]{1,0:T(8,128)(2,1)}), bf16[256,1024]{1,0:T(8,128)(2,1)}) %reduce-scatter.2.cloned.1.call-update) | async-done | bytes 524304 | tf_op jit(solution)/shard_map/reduce_scatter | solution.py:101
  211.7 13.4 %all_to_all.29 = bf16[8,32,1024]{2,1,0:T(8,128)(2,1)S(1)} all-to-all(bf16[8,32,1024]{2,1,0:T(8,128)(2,1)} %bitcast.34), channel_id=1, replica_groups=mesh['seq'=8,'chan'=4] {'seq'}, dimensions={0} | all-to-all | bytes 1048576 | tf_op jit(solution)/shard_map/all_to_all | solution.py:108
  225.1 0.3 copy.39
  225.3 0.4 all_to_all.25
  225.7 0.3 copy.40
  226.0 16.7 %all_to_all.30 = bf16[32,4,2048]{2,0,1:T(8,128)(2,1)S(1)} all-to-all(bf16[32,4,2048]{2,0,1:T(8,128)(2,1)S(1)} %copy.40), channel_id=1, replica_groups=mesh['seq'=8,'chan'=4] {'chan'}, dimensions={1} | all-to-all | bytes 1048576 | tf_op jit(solution)/shard_map/all_to_all | solution.py:107
  242.7 0.9 fusion.9
  (28 shorter events, 1.0 us)
Async XLA Ops:
  6.5 42.9 %all-gather.4.cloned.1.call-start = ((), (), s32[]{:S(2)}) async-start(), calls=%async_computation.3 | async-start | bytes 4718592 | tf_op jit(solution)/shard_map/all_gather | solution.py:69
  8.6 80.1 %all-gather.6.cloned.1.call-start = ((), (), s32[]{:S(2)}) async-start(), calls=%async_computation.4 | async-start | bytes 4718592 | tf_op jit(solution)/shard_map/all_gather | solution.py:70
  10.8 141.2 %all-gather.8.cloned.1.call-start = ((), (), s32[]{:S(2)}) async-start(), calls=%async_computation.5 | async-start | bytes 4718592 | tf_op jit(solution)/shard_map/all_gather | solution.py:96
  93.5 118.2 %reduce-scatter.2.cloned.1.call-start = ((), (), s32[]{:S(2)}) async-start(), calls=%async_computation.6 | async-start | bytes 2621440 | tf_op jit(solution)/shard_map/reduce_scatter | solution.py:101
  158.4 3.4 %copy-start.1 = (bf16[2048,1024]{1,0:T(8,128)(2,1)S(1)}, bf16[2048,1024]{1,0:T(8,128)(2,1)}, u32[]{:S(2)}) copy-start(bf16[2048,1024]{1,0:T(8,128)(2,1)} %param.13) | copy-start | bytes 12582916
  167.6 75.1 %copy-start = (bf16[128,2048]{1,0:T(8,128)(2,1)S(1)}, bf16[128,2048]{1,0:T(8,128)(2,1)}, u32[]{:S(2)}) copy-start(bf16[128,2048]{1,0:T(8,128)(2,1)} %param.12) | copy-start | bytes 1572868
Sparse Core Ops, SparseCore 0:
  9.2 40.1 all-gather.3
  51.3 37.4 all-gather.5
  93.6 58.2 all-gather.7
  167.8 43.8 reduce-scatter.1
where the time goes:
time: 251 us; the launch traced here: 250 us
  waiting for transfers between devices  179 us (71%)
  blocking collectives  30.1 us (12%)
  local copies, waits for them, and re-layouts  18.4 us (7%)
  between operations  13.2 us (5%)
  matrix products  7.06 us (3%)
    all_gather x1, waiting for transfers between devices, per_device(): gathered = lax.all_gather(local_context, 'seq', axis=0, tiled=True)  58.4 us
    reduce_scatter x1, waiting for transfers between devices, per_device(): lax.psum_scatter(jnp.dot(rows, out_weight, preferred_element_type=jnp.flo...  44 us
    all_gather x1, waiting for transfers between devices, per_device(): piece_values = lax.all_gather(value_proj, 'seq', axis=0, tiled=True)  39.3 us
    all_gather x1, waiting for transfers between devices, per_device(): piece_keys = lax.all_gather(key_proj, 'seq', axis=0, tiled=True)  37 us
    all_to_all x1, blocking collectives, per_device(): lax.all_to_all(lax.all_to_all(partial_sums.astype(jnp.bfloat16), 'seq', s...  16.7 us
    all_to_all x1, blocking collectives, per_device(): lax.all_to_all(partial_sums.astype(jnp.bfloat16), 'seq', split_axis=0, co...  13.4 us
    all_gather x1, local copies, waits for them, and re-layouts, per_device(): gathered = lax.all_gather(local_context, 'seq', axis=0, tiled=True)  6.53 us
    unnamed x7, local copies, waits for them, and re-layouts  6.22 us
  transfers between devices with their start and end apart: 4, of which 4 were waited for; matrix products, arithmetic and copies ran while one was open for 1% of the time, Pallas kernels for 0%

commit v1 on v0

--- a/solution.py
+++ b/solution.py
@@ -66,8 +66,15 @@
             for rows, first_pos in shaped
         )
     )
-    piece_keys = lax.all_gather(key_proj, "seq", axis=0, tiled=True)
-    piece_values = lax.all_gather(value_proj, "seq", axis=0, tiled=True)
+
+    def _state_plane(in_array, obj):
+        return jnp.split(
+            lax.all_gather(jnp.concatenate([in_array, obj], axis=1), "seq", tiled=True, axis=0),
+            [in_array.shape[1]],
+            axis=1,
+        )
+
+    piece_keys, piece_values = _state_plane(key_proj, value_proj)
     piece_rows = piece_keys.shape[0]
 
     def one_block(block_index, states):

time: 251 us -> 237 us (0.944)
  waiting for transfers between devices: 179 us -> 161 us
  local copies, waits for them, and re-layouts: 18.4 us -> 21.8 us
    all_gather x2 -> x1, waiting for transfers between devices: 76.3 us -> 58.2 us  [_state_plane(): lax.all_gather(jnp.concatenate([in_array, obj], axis=1), 'seq', tiled=Tru...]
    split x0 -> x1, local copies, waits for them, and re-layouts: none -> 5.9 us  [_state_plane(): jnp.split(lax.all_gather(jnp.concatenate([in_array, obj], axis=1), 'seq',...]
    unnamed x7 -> x9, local copies, waits for them, and re-layouts: 6.22 us -> 3.74 us
  transfers between devices with their start and end apart: 4 -> 3, of which waited for: 4 -> 3; matrix products, arithmetic and copies ran while one was open for 1% -> 0% of each run, Pallas kernels for 0% -> 0%
where the time goes in v1:
time: 237 us
  waiting for transfers between devices  161 us (68%)
  blocking collectives  30 us (13%)
  local copies, waits for them, and re-layouts  21.8 us (9%)
  between operations  13.2 us (6%)
  matrix products  7.06 us (3%)
  other arithmetic  3.28 us (1%)
    all_gather x1, waiting for transfers between devices, per_device(): gathered = lax.all_gather(local_context, 'seq', axis=0, tiled=True)  58.4 us
    all_gather x1, waiting for transfers between devices, _state_plane(): lax.all_gather(jnp.concatenate([in_array, obj], axis=1), 'seq', tiled=Tru...  58.2 us
    reduce_scatter x1, waiting for transfers between devices, per_device(): lax.psum_scatter(jnp.dot(rows, out_weight, preferred_element_type=jnp.flo...  44 us
    all_to_all x1, blocking collectives, per_device(): lax.all_to_all(lax.all_to_all(partial_sums.astype(jnp.bfloat16), 'seq', s...  16.7 us
    all_to_all x1, blocking collectives, per_device(): lax.all_to_all(partial_sums.astype(jnp.bfloat16), 'seq', split_axis=0, co...  13.4 us
    all_gather x1, local copies, waits for them, and re-layouts, per_device(): gathered = lax.all_gather(local_context, 'seq', axis=0, tiled=True)  6.53 us
    split x1, local copies, waits for them, and re-layouts, _state_plane(): jnp.split(lax.all_gather(jnp.concatenate([in_array, obj], axis=1), 'seq',...  5.9 us
    dot_general x1, matrix products, per_device(): jnp.dot(rows, out_weight, preferred_element_type=jnp.float32)  5.73 us
  transfers between devices with their start and end apart: 3, of which 3 were waited for; matrix products, arithmetic and copies ran while one was open for 0% of the time, Pallas kernels for 0%

profile of v1, /device:TPU:0, one launch (start us, length us, event | category | flops | bytes accessed | tf_op | source)
XLA Modules:
  0.0 236.5 jit_solution(5387086142434809409)
XLA Ops:
  6.5 1.4 copy.32
  7.9 1.3 copy.33
  9.2 1.1 pad_maximum_fusion
  11.0 58.2 %all-gather.3.cloned.1.call-done = bf16[1024,4096]{0,1:T(8,128)(2,1)} async-done(((bf16[128,4096]{0,1:T(8,128)(2,1)}), bf16[1024,4096]{0,1:T(8,128)(2,1)}) %all-gather.3.cloned.1.call-update) | async-done | bytes 8388624 | tf_op jit(solution)/shard_map/all_gather | solution.py:72
  69.2 5.9 %fusion.11 = (bf16[1024,2048]{0,1:T(8,128)(2,1)}, bf16[1024,2048]{0,1:T(8,128)(2,1)}) fusion(bf16[1024,4096]{0,1:T(8,128)(2,1)} %all-gather.3.cloned.1.call-done), kind=kLoop, calls=%fused_computation.24 | loop fusion | bytes 16777216 | tf_op jit(solution)/shard_map/split | solution.py:71
  75.2 3.3 %while.19 = (s32[]{:T(128)}, f32[16,128]{1,0:T(8,128)S(1)}, f32[16,128]{1,0:T(8,128)S(1)}, f32[16,128,128]{2,1,0:T(8,128)S(1)}, s32[]{:T(128)}, /*index=5*/s32[]...) while((s32[]{:T(128)}, f32[16,128]{1,0:T(8,128)S(1)}, ...), condition=%wide.region_5.6_spmd, body=%wide.region_0.5_spmd.sunk | while | flops 137122048 | bytes 9111853 | solution.py:95
  75.2 3.0 %conditional.2 = ((f32[16,128]{1,0:T(8,128)S(1)}, f32[16,128]{1,0:T(8,128)S(1)}, f32[16,128,128]{2,1,0:T(8,128)S(1)})) conditional(s32[]{:T(128)} %convert_element_type.63, (f32[16,128]{1,0:T(8,128)S(1)}, f32[16,128]{1,0:T(8,128)S(1)}, f32[16,128,128]{2,1,0:T(8,128)S(1)}) %tuple.62, (s32[]{:T(128)}, s32[]{:T(128)}, bf16[1024,2048]{0,1:T(8,128)(2,1)}, ...), branch_computations={%region_1.0_spmd, %region_2.4_spmd} | conditional | flops 137122048 | bytes 9111630 | solution.py:44
  75.3 1.3 constant_dynamic-slice_fusion
  76.7 0.5 fusion.10
  77.4 0.8 convolution_add_fusion
  78.6 0.3 copy.36
  78.9 0.9 divide_convert_fusion
  79.9 58.4 %all-gather.5.cloned.1.call-done = bf16[1024,2048]{0,1:T(8,128)(2,1)} async-done(((bf16[128,2048]{0,1:T(8,128)(2,1)}), bf16[1024,2048]{0,1:T(8,128)(2,1)}) %all-gather.5.cloned.1.call-update) | async-done | bytes 4194320 | tf_op jit(solution)/shard_map/all_gather | solution.py:103
  138.3 6.5 %copy.37 = bf16[1024,2048]{1,0:T(8,128)(2,1)} copy(bf16[1024,2048]{0,1:T(8,128)(2,1)} %all-gather.5.cloned.1.call-done) | data formatting | bytes 8388608 | tf_op jit(solution)/shard_map/all_gather | solution.py:103
  144.8 2.7 %copy.38 = bf16[4,8,32,2048]{3,2,1,0:T(8,128)(2,1)S(1)} copy(bf16[4,8,32,2048]{3,2,0,1:T(8,128)(2,1)} %bitcast.29) | data formatting | bytes 8388608 | tf_op jit(solution)/shard_map/transpose | solution.py:107
  147.5 0.8 copy-done.2
  148.3 5.7 %convolution_convert_fusion = bf16[1024,1024]{1,0:T(8,128)(2,1)} fusion(bf16[1024,2048]{1,0:T(8,128)(2,1)S(1)} %bitcast.30, bf16[2048,1024]{1,0:T(8,128)(2,1)S(1)} %copy-done.2), kind=kOutput, calls=%fused_computation.18 | convolution fusion | flops 4296015872 | bytes 10485760 | tf_op jit(solution)/shard_map/dot_general | solution.py:109
  154.0 44.0 %reduce-scatter.2.cloned.1.call-done = bf16[256,1024]{1,0:T(8,128)(2,1)} async-done(((bf16[1024,1024]{1,0:T(8,128)(2,1)}), bf16[256,1024]{1,0:T(8,128)(2,1)}) %reduce-scatter.2.cloned.1.call-update) | async-done | bytes 524304 | tf_op jit(solution)/shard_map/reduce_scatter | solution.py:108
  198.1 13.4 %all_to_all.29 = bf16[8,32,1024]{2,1,0:T(8,128)(2,1)S(1)} all-to-all(bf16[8,32,1024]{2,1,0:T(8,128)(2,1)} %bitcast.34), channel_id=1, replica_groups=mesh['seq'=8,'chan'=4] {'seq'}, dimensions={0} | all-to-all | bytes 1048576 | tf_op jit(solution)/shard_map/all_to_all | solution.py:115
  211.4 0.3 copy.39
  211.7 0.4 all_to_all.25
  212.1 0.3 copy.40
  212.4 16.7 %all_to_all.30 = bf16[32,4,2048]{2,0,1:T(8,128)(2,1)S(1)} all-to-all(bf16[32,4,2048]{2,0,1:T(8,128)(2,1)S(1)} %copy.40), channel_id=1, replica_groups=mesh['seq'=8,'chan'=4] {'chan'}, dimensions={1} | all-to-all | bytes 1048576 | tf_op jit(solution)/shard_map/all_to_all | solution.py:114
  229.1 0.9 fusion.9
  (29 shorter events, 1.2 us)
Async XLA Ops:
  6.5 3.9 %copy-start.1 = (bf16[128,2048]{1,0:T(8,128)(2,1)S(1)}, bf16[128,2048]{1,0:T(8,128)(2,1)}, u32[]{:S(2)}) copy-start(bf16[128,2048]{1,0:T(8,128)(2,1)} %param.9) | copy-start | bytes 1572868
  6.5 62.7 %all-gather.3.cloned.1.call-start = ((), (), s32[]{:S(2)}) async-start(), calls=%async_computation.3 | async-start | bytes 9437184 | tf_op jit(solution)/shard_map/all_gather | solution.py:72
  10.4 127.9 %all-gather.5.cloned.1.call-start = ((), (), s32[]{:S(2)}) async-start(), calls=%async_computation.4 | async-start | bytes 4718592 | tf_op jit(solution)/shard_map/all_gather | solution.py:103
  79.9 118.2 %reduce-scatter.2.cloned.1.call-start = ((), (), s32[]{:S(2)}) async-start(), calls=%async_computation.5 | async-start | bytes 2621440 | tf_op jit(solution)/shard_map/reduce_scatter | solution.py:108
  144.8 3.4 %copy-start.2 = (bf16[2048,1024]{1,0:T(8,128)(2,1)S(1)}, bf16[2048,1024]{1,0:T(8,128)(2,1)}, u32[]{:S(2)}) copy-start(bf16[2048,1024]{1,0:T(8,128)(2,1)} %param.13) | copy-start | bytes 12582916
  154.0 75.1 %copy-start = (bf16[128,2048]{1,0:T(8,128)(2,1)S(1)}, bf16[128,2048]{1,0:T(8,128)(2,1)}, u32[]{:S(2)}) copy-start(bf16[128,2048]{1,0:T(8,128)(2,1)} %param.12) | copy-start | bytes 1572868
Sparse Core Ops, SparseCore 0:
  10.5 58.6 all-gather.2
  80.0 58.2 all-gather.4
  154.1 43.8 reduce-scatter.1
